TPU v7x, 256 devices: a whole 4x4x8 slice. The times are simulated.
256 devices in a mesh: batch: 16 (over y_hi, z), gx: 4 (over y_lo, core), gy: 4 (over x).
Axes of the slice: x: 4, y: 4 (y_hi: 2, y_lo: 2; y = y_hi * 2 + y_lo), z: 8, core: 2. Of those that a mesh axis runs over, the one named last changes fastest.
Arguments:
- features: bfloat16 [1024, 64, 4, 256], P(('batch', 'gx'), 'gy'), parts along dimension 0, may hold values from -6 to 6
- conv_weight: bfloat16 [6912, 256], replicated, may hold values from -0.078125 to 0.078125
- down_weight: bfloat16 [2048, 512], replicated, may hold values from -0.125 to 0.125
- norm_gain: float32 [512], replicated, may hold values from 0.1 to 1.9
- qkv_weight: bfloat16 [512, 1536], replicated, may hold values from -0.25 to 0.25
- out_weight: bfloat16 [512, 512], replicated, may hold values from -0.25 to 0.25
- upstream: bfloat16 [512, 32, 2, 512], P(('batch', 'gx'), 'gy'), parts along dimension 0, may hold values from -6 to 6
Outputs:
- grad_features: bfloat16 [1024, 64, 4, 256], P(('batch', 'gx'), 'gy'), parts along dimension 0
- grad_conv: bfloat16 [110592, 256], P(('batch', 'gx', 'gy')), parts along dimension 0
- grad_down: bfloat16 [32768, 512], P(('batch', 'gx', 'gy')), parts along dimension 0
- grad_gain: float32 [8192], P(('batch', 'gx', 'gy')), parts along dimension 0
- grad_qkv: bfloat16 [8192, 1536], P(('batch', 'gx', 'gy')), parts along dimension 0
- grad_out: bfloat16 [8192, 512], P(('batch', 'gx', 'gy')), parts along dimension 0
There are 16 independent parts, one for each index of `batch`. A program takes and returns all parts, laid end to end along the dimension named above; an argument that names none is the same for every part. Nothing has to cross between parts.
All inputs are finite; a program needn't handle non-finite values.
Results may differ from a plain program's by a relative error of at most 0.02.
Values may be sent and summed in bfloat16 or wider, within the bound.
No kernel may reach another device: no remote copies, remote signals or barrier semaphores. Data moves between devices by JAX's collectives and lax.ppermute only.
A program may use at most 128 MiB of HBM per device.

v0:
```python
import jax
import jax.numpy as jnp
from jax import lax
from jax.sharding import PartitionSpec as P

H = 8
HD = 64
precise = lax.Precision.HIGHEST


def padded_2(block, sides, width):
    for axis, dim in sides:
        count = lax.axis_size(axis)
        forward = [(i, i + 1) for i in range(count - 1)]
        backward = [(target, source) for source, target in forward]
        low = lax.ppermute(
            lax.slice_in_dim(block, block.shape[dim] - width, None, axis=dim), axis, forward
        )
        high = lax.ppermute(lax.slice_in_dim(block, 0, width, axis=dim), axis, backward)
        block = jnp.concatenate([low, block, high], axis=dim)
    return block


def to_tokens(volume):
    extent_x, extent_y, extent_z, channels = volume.shape
    grid = volume.reshape(extent_x // 2, 2, extent_y // 2, 2, extent_z // 2, 2, channels)
    grid = grid.transpose(0, 2, 4, 1, 3, 5, 6)
    return grid.reshape(extent_x * extent_y * extent_z // 8, 8 * channels)


def from_tokens(matrix, extent_x, extent_y, extent_z):
    channels = matrix.shape[1] // 8
    grid = matrix.reshape(extent_x // 2, extent_y // 2, extent_z // 2, 2, 2, 2, channels)
    grid = grid.transpose(0, 3, 1, 4, 2, 5, 6)
    return grid.reshape(extent_x, extent_y, extent_z, channels)


def gather_patches(padded, extent_x, extent_y, extent_z, flipped):
    channels = padded.shape[3]
    pieces = []
    for offset_x in range(3):
        for offset_y in range(3):
            for offset_z in range(3):
                start_x = 2 - offset_x if flipped else offset_x
                start_y = 2 - offset_y if flipped else offset_y
                start_z = 2 - offset_z if flipped else offset_z
                pieces.append(
                    padded[
                        start_x : start_x + extent_x,
                        start_y : start_y + extent_y,
                        start_z : start_z + extent_z,
                    ]
                )
    joined = jnp.concatenate(pieces, axis=3)
    return joined.reshape(extent_x * extent_y * extent_z, 27 * channels)


def local(features, conv_weight, down_weight, norm_gain, qkv_weight, out_weight, upstream):
    extent_x, extent_y, extent_z, channels = features.shape
    model_width = out_weight.shape[0]
    voxels = extent_x * extent_y * extent_z
    score_scale = HD ** (-0.5)
    padded = padded_2(features, (("gx", 0), ("gy", 1)), 1)
    padded = jnp.pad(padded, ((0, 0), (0, 0), (1, 1), (0, 0)))
    patches = gather_patches(padded, extent_x, extent_y, extent_z, False)
    hidden = jnp.dot(patches, conv_weight, preferred_element_type=jnp.float32)
    gate_sig = jax.nn.sigmoid(hidden)
    activation = (hidden * gate_sig).astype(jnp.bfloat16)
    tokens_in = to_tokens(activation.reshape(extent_x, extent_y, extent_z, channels))
    tok_count = tokens_in.shape[0]
    trunk_rows = jnp.dot(tokens_in, down_weight, preferred_element_type=jnp.float32)
    mean_rows = jnp.mean(trunk_rows, axis=-1, keepdims=True)
    centred = trunk_rows - mean_rows
    inverse_std = lax.rsqrt(jnp.mean(centred * centred, axis=-1, keepdims=True) + 1e-05)
    normed = centred * inverse_std
    normed_b = (normed * norm_gain).astype(jnp.bfloat16)
    qkv_rows = jnp.dot(normed_b, qkv_weight, preferred_element_type=jnp.float32).astype(
        jnp.bfloat16
    )
    queries = qkv_rows[:, :model_width]
    local_keys = qkv_rows[:, model_width : 2 * model_width]
    local_values = qkv_rows[:, 2 * model_width :]
    all_keys, all_values = (
        lax.all_gather(local_keys, ("gx", "gy"), axis=0, tiled=True),
        lax.all_gather(local_values, ("gx", "gy"), axis=0, tiled=True),
    )
    queries_h = queries.reshape(tok_count, H, HD)
    keys_h = all_keys.reshape(-1, H, HD)
    values_h = all_values.reshape(-1, H, HD)
    scores = (
        jnp.einsum("ihe,jhe->hij", queries_h, keys_h, preferred_element_type=jnp.float32)
        * score_scale
    )
    exp_scores = jnp.exp(scores)
    totals = jnp.sum(exp_scores, axis=-1)
    attn_probs = exp_scores / totals[:, :, None]
    probs_b = attn_probs.astype(jnp.bfloat16)
    attended = jnp.einsum("hij,jhe->ihe", probs_b, values_h, preferred_element_type=jnp.float32)
    attended = attended.reshape(tok_count, model_width).astype(jnp.bfloat16)
    cotangent = upstream.reshape(tok_count, model_width)
    cot_float = cotangent.astype(jnp.float32)
    out_part = jnp.einsum("td,te->de", attended, cotangent, preferred_element_type=jnp.float32)
    d_attended = jnp.dot(cotangent, out_weight.T, preferred_element_type=jnp.float32).astype(
        jnp.bfloat16
    )
    d_att_h = d_attended.reshape(tok_count, H, HD)
    d_probs = jnp.einsum("ihe,jhe->hij", d_att_h, values_h, preferred_element_type=jnp.float32)
    d_probs = d_probs.astype(jnp.bfloat16).astype(jnp.float32)
    row_delta = jnp.sum(attn_probs * d_probs, axis=-1)
    d_scores = attn_probs * (d_probs - row_delta[:, :, None])
    d_queries = (
        jnp.einsum(
            "hij,jhe->ihe", d_scores, keys_h, precision=precise, preferred_element_type=jnp.float32
        )
        * score_scale
    )
    key_term = (
        jnp.einsum(
            "hij,ihe->jhe",
            d_scores,
            queries_h,
            precision=precise,
            preferred_element_type=jnp.float32,
        )
        * score_scale
    )
    value_term = jnp.einsum("hij,ihe->jhe", probs_b, d_att_h, preferred_element_type=jnp.float32)
    key_sums = lax.psum_scatter(
        jnp.concatenate(
            [
                key_term.reshape(tok_count * lax.axis_size(("gx", "gy")), model_width),
                value_term.reshape(tok_count * lax.axis_size(("gx", "gy")), model_width),
            ],
            axis=1,
        ).astype(jnp.bfloat16),
        ("gx", "gy"),
        scatter_dimension=0,
        tiled=True,
    ).astype(jnp.float32)
    d_keys = key_sums[:, :model_width].astype(jnp.bfloat16)
    d_values = key_sums[:, model_width:].astype(jnp.bfloat16)
    d_qkv = jnp.concatenate(
        [d_queries.reshape(tok_count, model_width).astype(jnp.bfloat16), d_keys, d_values], axis=1
    )
    qkv_part = jnp.einsum("td,te->de", normed_b, d_qkv, preferred_element_type=jnp.float32)
    d_normed = (
        jnp.dot(d_qkv, qkv_weight.T, preferred_element_type=jnp.float32)
        .astype(jnp.bfloat16)
        .astype(jnp.float32)
    )
    d_hat = d_normed * norm_gain
    gain_part = jnp.sum(d_normed * normed, axis=0)
    gain_sum = lax.psum_scatter(gain_part, ("gx", "gy"), scatter_dimension=0, tiled=True)
    d_trunk = cot_float + inverse_std * (
        d_hat
        - jnp.mean(d_hat, axis=-1, keepdims=True)
        - normed * jnp.mean(d_hat * normed, axis=-1, keepdims=True)
    )
    down_part = jnp.einsum(
        "tr,td->rd", tokens_in, d_trunk, precision=precise, preferred_element_type=jnp.float32
    )
    d_activation = jnp.dot(
        d_trunk, down_weight.T, precision=precise, preferred_element_type=jnp.float32
    ).astype(jnp.bfloat16)
    d_act_grid = (
        from_tokens(d_activation, extent_x, extent_y, extent_z)
        .reshape(voxels, channels)
        .astype(jnp.float32)
    )
    d_hidden = (d_act_grid * gate_sig * (1.0 + hidden * (1.0 - gate_sig))).astype(jnp.bfloat16)
    conv_part = jnp.einsum("vr,vc->rc", patches, d_hidden, preferred_element_type=jnp.float32)
    d_padded = padded_2(
        d_hidden.reshape(extent_x, extent_y, extent_z, channels), (("gx", 0), ("gy", 1)), 1
    )
    d_padded = jnp.pad(d_padded, ((0, 0), (0, 0), (1, 1), (0, 0)))
    d_patches = gather_patches(d_padded, extent_x, extent_y, extent_z, True)
    conv_flip = (
        conv_weight.reshape(27, channels, channels)
        .transpose(0, 2, 1)
        .reshape(27 * channels, channels)
    )
    grad_features = jnp.dot(d_patches, conv_flip, preferred_element_type=jnp.float32)
    grad_features = grad_features.reshape(extent_x, extent_y, extent_z, channels).astype(
        jnp.bfloat16
    )
    conv_sum, down_sum, qkv_sum, out_sum = (
        lax.psum_scatter(
            conv_part.astype(jnp.bfloat16), ("gx", "gy"), scatter_dimension=0, tiled=True
        ).astype(jnp.float32),
        lax.psum_scatter(
            down_part.astype(jnp.bfloat16), ("gx", "gy"), scatter_dimension=0, tiled=True
        ).astype(jnp.float32),
        lax.psum_scatter(
            qkv_part.astype(jnp.bfloat16), ("gx", "gy"), scatter_dimension=0, tiled=True
        ).astype(jnp.float32),
        lax.psum_scatter(
            out_part.astype(jnp.bfloat16), ("gx", "gy"), scatter_dimension=0, tiled=True
        ).astype(jnp.float32),
    )
    return (
        grad_features,
        conv_sum.astype(jnp.bfloat16),
        down_sum.astype(jnp.bfloat16),
        gain_sum,
        qkv_sum.astype(jnp.bfloat16),
        out_sum.astype(jnp.bfloat16),
    )


def solution(mesh):
    placed = (
        P(("batch", "gx"), "gy", None, None),
        P(),
        P(),
        P(),
        P(),
        P(),
        P(("batch", "gx"), "gy", None, None),
    )
    return jax.shard_map(
        local,
        mesh=mesh,
        in_specs=placed,
        out_specs=(
            P(("batch", "gx"), "gy", None, None),
            P(("batch", "gx", "gy"), None),
            P(("batch", "gx", "gy"), None),
            P(("batch", "gx", "gy")),
            P(("batch", "gx", "gy"), None),
            P(("batch", "gx", "gy"), None),
        ),
        check_vma=False,
    )
```

profile of v0, /device:TPU:16, one launch (start us, length us, event | category | flops | bytes accessed | tf_op | source)
XLA Modules:
  0.0 585.7 jit_solution(17432155267392307056)
XLA Ops:
  8.2 1.7 collective-permute-start
  9.9 1.3 collective-permute-start.1
  11.3 1.4 constant_dynamic-update-slice_fusion.1
  12.6 1.5 collective-permute-done.1
  14.1 3.4 collective-permute-start.2
  17.6 1.3 collective-permute-start.3
  19.2 4.2 collective-permute-done.3
  25.1 1.2 fusion.45
  27.4 1.1 slice_dynamic-update-slice_fusion.33
  28.6 2.1 fusion.61
  30.7 1.1 slice_dynamic-update-slice_fusion.32
  33.0 1.2 fusion.41
  34.2 1.2 slice_dynamic-update-slice_fusion.30
  36.4 1.1 fusion.43
  37.6 1.1 slice_dynamic-update-slice_fusion.28
  40.9 1.1 slice_dynamic-update-slice_fusion.26
  43.2 1.2 fusion.39
  44.3 1.2 slice_dynamic-update-slice_fusion.24
  45.5 1.2 slice_dynamic-update-slice_fusion.23
  46.7 1.1 fusion.60
  47.8 1.2 slice_dynamic-update-slice_fusion.22
  51.3 1.1 slice_dynamic-update-slice_fusion.20
  53.5 1.2 fusion.58
  54.7 1.2 slice_dynamic-update-slice_fusion.18
  55.8 22.7 %reshape.89 = bf16[1024,6912]{1,0:T(8,128)(2,1)} reshape(bf16[16,16,4,6912]{3,2,1,0:T(4,128)(2,1)} %slice_dynamic-update-slice_fusion.18) | data formatting | bytes 28311552 | tf_op jit(solution)/shard_map/reshape | solution.py:55
  78.6 10.9 %multiply_convert_fusion.2 = (bf16[1024,256]{1,0:T(8,128)(2,1)S(1)}, f32[1024,256]{1,0:T(8,128)}) fusion(bf16[1024,6912]{1,0:T(8,128)(2,1)} %reshape.89, bf16[6912,256]{1,0:T(8,128)(2,1)} %param.8), kind=kOutput, calls=%fused_computation.54 | convolution fusion | flops 3625189376 | bytes 19267584 | tf_op jit(solution)/shard_map/dot_general | solution.py:66
  91.2 1.8 convolution_convert_fusion.6
  95.5 1.3 convolution_convert_fusion.9
  97.2 49.0 %all-gather.3.cloned.1.call-done = bf16[2048,512]{1,0:T(8,128)(2,1)} async-done(((bf16[128,512]{1,0:T(8,128)(2,1)}), bf16[2048,512]{1,0:T(8,128)(2,1)}) %all-gather.3.cloned.1.call-update) | async-done | bytes 2097168 | tf_op jit(solution)/shard_map/all_gather | solution.py:84
  146.2 4.1 copy.45
  150.3 3.1 fusion.3
  153.4 3.3 copy-done.2
  156.7 3.0 convolution_convert_fusion.4
  159.7 39.5 %all-gather.5.cloned.1.call-done = bf16[2048,512]{1,0:T(8,128)(2,1)} async-done(((bf16[128,512]{1,0:T(8,128)(2,1)}), bf16[2048,512]{1,0:T(8,128)(2,1)}) %all-gather.5.cloned.1.call-update) | async-done | bytes 2097168 | tf_op jit(solution)/shard_map/all_gather | solution.py:85
  199.2 4.0 copy.48
  203.1 6.7 %fusion = (f32[8,128]{1,0:T(8,128)S(1)}, bf16[8,128,2048]{2,1,0:T(8,128)(2,1)S(1)}) fusion(f32[8,128]{1,0:T(8,128)S(1)} %get-tuple-element.44, f32[8,128,2048]{2,1,0:T(8,128)} %copy-done.2, bf16[128,8,64]{0,2,1:T(8,128)(2,1)S(1)} %bitcast.71, bf16[2048,8,64]{0,2,1:T(8,128)(2,1)} %bitcast.61), kind=kOutput, calls=%fused_computation.3 | convolution fusion | flops 281017344 | bytes 14819328 | tf_op jit(solution)/shard_map/ihe,jhe->hij/dot_general | solution.py:107
  209.9 5.9 %multiply_convert_fusion = bf16[8,64,2048]{2,1,0:T(8,128)(2,1)S(1)} fusion(bf16[128,8,64]{0,2,1:T(8,128)(2,1)S(1)} %bitcast.67, bf16[8,128,2048]{2,1,0:T(8,128)(2,1)S(1)} %get-tuple-element.47, f32[8,128]{1,0:T(8,128)S(1)} %get-tuple-element.46, f32[8,128,2048]{2,1,0:T(8,128)S(1)} %copy-done.3, f32[8,128]{1,0:T(8,128)S(1)} %get-tuple-element.44), kind=kOutput, calls=%fused_computation.11 | convolution fusion | flops 1623195648 | bytes 14819328 | tf_op jit(solution)/shard_map/hij,ihe->jhe/dot_general | solution.py:118
  215.8 2.5 pad_maximum_fusion
  218.3 6.4 %copy.59 = bf16[2048,1024]{1,0:T(8,128)(2,1)} copy(bf16[2048,1024]{0,1:T(8,128)(2,1)} %pad_maximum_fusion) | data formatting | bytes 8388608
  224.8 5.7 fusion.31
  231.9 11.9 %fusion.34 = bf16[8,64,128]{2,1,0:T(8,128)(2,1)S(1)} fusion(bf16[2048,8,64]{0,2,1:T(8,128)(2,1)} %bitcast.57, bf16[8,128,2048]{2,1,0:T(8,128)(2,1)} %copy-done.14, f32[8,128]{1,0:T(8,128)S(1)} %get-tuple-element.46, f32[8,128,2048]{2,1,0:T(8,128)} %copy-done.2, f32[8,128]{1,0:T(8,128)S(1)} %get-tuple-element.44), kind=kOutput, calls=%fused_computation.49 | convolution fusion | flops 1621229568 | bytes 14819328 | tf_op jit(solution)/shard_map/hij,jhe->ihe/dot_general | solution.py:112
  243.8 56.7 %reduce-scatter.16.cloned.1.call-done = bf16[128,1024]{1,0:T(8,128)(2,1)} async-done(((bf16[2048,1024]{1,0:T(8,128)(2,1)}), bf16[128,1024]{1,0:T(8,128)(2,1)}) %reduce-scatter.16.cloned.1.call-update) | async-done | bytes 262160
  301.7 1.8 convolution_convert_fusion.3
  303.6 2.8 multiply_reduce_fusion
  306.4 3.3 convolution_convert_fusion.2
  310.2 3.1 fusion.14
  313.4 1.9 reshape.101
  315.3 2.7 copy.66
  318.0 1.9 reshape.100
  319.9 1.6 multiply_convert_fusion.1
  322.3 1.3 collective-permute-start.4
  323.6 5.7 copy.56
  330.6 2.0 reshape.97
  332.7 1.3 collective-permute-start.5
  334.0 1.2 fusion.70
  335.2 1.9 collective-permute-done.5
  337.8 1.3 collective-permute-start.6
  339.1 1.3 collective-permute-start.7
  340.4 10.7 %convolution_convert_fusion = bf16[6912,256]{1,0:T(8,128)(2,1)} fusion(bf16[1024,6912]{1,0:T(8,128)(2,1)} %reshape.89, bf16[1024,256]{1,0:T(8,128)(2,1)} %copy-done.6), kind=kOutput, calls=%fused_computation.2 | convolution fusion | flops 3625648128 | bytes 18219008 | tf_op jit(solution)/shard_map/vr,vc->rc/dot_general | solution.py:171
  351.2 30.0 %all-reduce.2 = f32[512]{0:T(512)S(1)} all-reduce(f32[512]{0:T(512)S(1)} %copy-done.12), channel_id=5, replica_groups=mesh['batch'=16,'gx'=4,'gy'=4] {'gx','gy'}, use_global_device_ids=true, to_apply=%region_10.11.clone | all-reduce | flops 512 | bytes 4096
  387.1 3.8 convolution_convert_fusion.7
  392.0 42.7 %reduce-scatter.12.cloned.1.call-done = bf16[32,1536]{1,0:T(8,128)(2,1)} async-done(((bf16[512,1536]{1,0:T(8,128)(2,1)}), bf16[32,1536]{1,0:T(8,128)(2,1)}) %reduce-scatter.12.cloned.1.call-update) | async-done | bytes 98320 | tf_op jit(solution)/shard_map/reduce_scatter | solution.py:193
  434.7 69.8 %reduce-scatter.10.cloned.1.call-done = bf16[128,512]{1,0:T(8,128)(2,1)} async-done(((bf16[2048,512]{1,0:T(8,128)(2,1)}), bf16[128,512]{1,0:T(8,128)(2,1)}) %reduce-scatter.10.cloned.1.call-update) | async-done | bytes 131088 | tf_op jit(solution)/shard_map/reduce_scatter | solution.py:190
  504.5 74.1 %reduce-scatter.8.cloned.1.call-done = bf16[432,256]{1,0:T(8,128)(2,1)} async-done(((bf16[6912,256]{1,0:T(8,128)(2,1)}), bf16[432,256]{1,0:T(8,128)(2,1)}) %reduce-scatter.8.cloned.1.call-update) | async-done | bytes 221200 | tf_op jit(solution)/shard_map/reduce_scatter | solution.py:187
  (117 shorter events, 29.6 us)
Async XLA Ops:
  7.2 83.3 %copy-start = (bf16[2048,512]{1,0:T(8,128)(2,1)S(1)}, bf16[2048,512]{1,0:T(8,128)(2,1)}, u32[]{:S(2)}) copy-start(bf16[2048,512]{1,0:T(8,128)(2,1)} %param.9) | copy-start | bytes 6291460
  7.2 139.0 %all-gather.3.cloned.1.call-start = ((), (), s32[]{:S(2)}) async-start(), calls=%async_computation.5 | async-start | bytes 2228224 | tf_op jit(solution)/shard_map/all_gather | solution.py:84
  8.2 3.1 collective-permute-start
  9.9 4.2 collective-permute-start.1
  11.2 28.6 %copy-start.1 = (bf16[16,16,4,256]{3,2,1,0:T(4,128)(2,1)S(1)}, bf16[16,16,4,256]{3,2,1,0:T(4,128)(2,1)}, u32[]{:S(2)}) copy-start(bf16[16,16,4,256]{3,2,1,0:T(4,128)(2,1)} %param.7) | copy-start | bytes 1572868
  14.1 5.0 collective-permute-start.2
  17.6 5.9 collective-permute-start.3
  78.6 12.6 %copy-start.10 = (f32[512]{0:T(512)S(1)}, f32[512]{0:T(512)}, u32[]{:S(2)}) copy-start(f32[512]{0:T(512)} %param.10) | copy-start | bytes 6148
  93.8 105.4 %all-gather.5.cloned.1.call-start = ((), (), s32[]{:S(2)}) async-start(), calls=%async_computation.6 | async-start | bytes 2228224 | tf_op jit(solution)/shard_map/all_gather | solution.py:85
  94.5 206.1 %reduce-scatter.16.cloned.1.call-start = ((), (), s32[]{:S(2)}) async-start(), calls=%async_computation.11 | async-start | bytes 4456448
  153.4 3.3 copy-start.2
  203.1 6.8 %copy-start.3 = (f32[8,128,2048]{2,1,0:T(8,128)S(1)}, f32[8,128,2048]{2,1,0:T(8,128)}, u32[]{:S(2)}) copy-start(f32[8,128,2048]{2,1,0:T(8,128)} %copy-done.2) | copy-start | bytes 25165828
  209.9 5.9 %copy-start.14 = (bf16[8,128,2048]{2,1,0:T(8,128)(2,1)}, bf16[8,128,2048]{2,1,0:T(8,128)(2,1)S(1)}, u32[]{:S(2)}) copy-start(bf16[8,128,2048]{2,1,0:T(8,128)(2,1)S(1)} %get-tuple-element.47) | copy-start | bytes 12582916
  209.9 5.9 %copy-start.7 = (bf16[8,64,2048]{2,1,0:T(8,128)(2,1)S(1)}, bf16[8,64,2048]{2,1,0:T(8,128)(2,1)}, u32[]{:S(2)}) copy-start(bf16[8,64,2048]{2,1,0:T(8,128)(2,1)} %convolution_convert_fusion.4) | copy-start | bytes 6291460
  224.8 167.3 %reduce-scatter.14.cloned.1.call-start = ((), (), s32[]{:S(2)}) async-start(), calls=%async_computation.10 | async-start | bytes 557056 | tf_op jit(solution)/shard_map/reduce_scatter | solution.py:196
  231.7 203.1 %reduce-scatter.12.cloned.1.call-start = ((), (), s32[]{:S(2)}) async-start(), calls=%async_computation.9 | async-start | bytes 1671168 | tf_op jit(solution)/shard_map/reduce_scatter | solution.py:193
  243.8 59.7 %copy-start.9 = (bf16[8,64,128]{2,1,0:T(8,128)(2,1)}, bf16[8,64,128]{2,1,0:T(8,128)(2,1)S(1)}, u32[]{:S(2)}) copy-start(bf16[8,64,128]{2,1,0:T(8,128)(2,1)S(1)} %fusion.34) | copy-start | bytes 393220
  303.6 201.0 %reduce-scatter.10.cloned.1.call-start = ((), (), s32[]{:S(2)}) async-start(), calls=%async_computation.8 | async-start | bytes 2228224 | tf_op jit(solution)/shard_map/reduce_scatter | solution.py:190
  306.4 3.4 copy-start.8
  306.4 3.4 copy-start.11
  309.8 268.8 %reduce-scatter.8.cloned.1.call-start = ((), (), s32[]{:S(2)}) async-start(), calls=%async_computation.7 | async-start | bytes 3760128 | tf_op jit(solution)/shard_map/reduce_scatter | solution.py:187
  313.4 16.0 %copy-start.13 = (u32[256]{0:T(256)S(1)}, u32[256]{0:T(256)}, u32[]{:S(2)}) copy-start(u32[256]{0:T(256)} %constant.27) | copy-start | bytes 3076
  321.5 0.8 copy-start.6
  322.3 11.6 %collective-permute-start.4 = (bf16[1,16,4,256]{3,1,2,0:T(8,128)(2,1)S(1)}, bf16[1,16,4,256]{3,1,2,0:T(8,128)(2,1)S(1)}, u32[]{:S(2)}, u32[]{:S(2)}) collective-permute-start(bf16[1,16,4,256]{3,1,2,0:T(8,128)(2,1)S(1)} %copy.50), channel_id=1, source_target_pairs={{0,4},{4,8},{8,12},{1,5},{5,9},{9,13},{2,6},{6,10},{10,14},{3,7},{... | collective-permute-start | bytes 98312 | tf_op jit(solution)/shard_map/ppermute | solution.py:16
  332.7 4.4 collective-permute-start.5
  337.8 44.0 %collective-permute-start.6 = (bf16[18,1,4,256]{3,1,2,0:T(2,128)(2,1)}, bf16[18,1,4,256]{3,1,2,0:T(2,128)(2,1)S(1)}, u32[]{:S(2)}, u32[]{:S(2)}) collective-permute-start(bf16[18,1,4,256]{3,1,2,0:T(2,128)(2,1)} %get-tuple-element.27), channel_id=1, source_target_pairs={{0,1},{1,2},{2,3},{4,5},{5,6},{6,7},{8,9},{9,10},{10,11},{12,13},{... | collective-permute-start | bytes 110600 | tf_op jit(solution)/shard_map/ppermute | solution.py:16
  339.1 12.1 %copy-start.12 = (f32[512]{0:T(512)S(1)}, f32[512]{0:T(512)}, u32[]{:S(2)}) copy-start(f32[512]{0:T(512)} %get-tuple-element.24) | copy-start | bytes 6148
  339.1 42.7 %collective-permute-start.7 = (bf16[18,1,4,256]{3,1,2,0:T(2,128)(2,1)S(1)}, bf16[18,1,4,256]{3,1,2,0:T(2,128)(2,1)S(1)}, u32[]{:S(2)}, u32[]{:S(2)}) collective-permute-start(bf16[18,1,4,256]{3,1,2,0:T(2,128)(2,1)S(1)} %get-tuple-element.28), channel_id=1, source_target_pairs={{1,0},{2,1},{3,2},{5,4},{6,5},{7,6},{9,8},{10,9},{11,10},{13,12},{... | collective-permute-start | bytes 110600 | tf_op jit(solution)/shard_map/ppermute | solution.py:19
  381.2 3.7 copy-start.4
  384.5 2.6 copy-start.5
Sparse Core Ops, SparseCore 0:
  93.9 52.2 all-gather.2
  148.6 50.5 all-gather.4
  224.9 75.6 reduce-scatter.15
  303.5 62.8 reduce-scatter.13
  369.4 65.2 reduce-scatter.11
  437.7 66.8 reduce-scatter.9
  507.7 70.9 reduce-scatter.7
where the time goes:
time: 593 us; the launch traced here: 586 us
  waiting for transfers between devices  341 us (58%)
  local copies, waits for them, and re-layouts  90.4 us (15%)
  matrix products  77.6 us (13%)
  blocking collectives  30 us (5%)
  other arithmetic  17.6 us (3%)
  between operations  15.6 us (3%)
  starting transfers between devices  13.8 us (2%)
    reduce_scatter x1, waiting for transfers between devices, local(): lax.psum_scatter(conv_part.astype(jnp.bfloat16), ('gx', 'gy'), scatter_di...  74.1 us
    reduce_scatter x1, waiting for transfers between devices, local(): lax.psum_scatter(down_part.astype(jnp.bfloat16), ('gx', 'gy'), scatter_di...  69.8 us
    unnamed x8, waiting for transfers between devices  57.5 us
    all_gather x1, waiting for transfers between devices, local(): lax.all_gather(local_keys, ('gx', 'gy'), axis=0, tiled=True)  49 us
    reduce_scatter x1, waiting for transfers between devices, local(): lax.psum_scatter(qkv_part.astype(jnp.bfloat16), ('gx', 'gy'), scatter_dim...  42.7 us
    all_gather x1, waiting for transfers between devices, local(): lax.all_gather(local_values, ('gx', 'gy'), axis=0, tiled=True)  39.5 us
    unnamed x74, local copies, waits for them, and re-layouts  38.3 us
    unnamed x1, blocking collectives  30 us
  transfers between devices with their start and end apart: 15, of which 10 were waited for; matrix products, arithmetic and copies ran while one was open for 14% of the time, Pallas kernels for 0%

commit v1 on v0

--- a/solution.py
+++ b/solution.py
@@ -82,7 +82,12 @@
     local_values = qkv_rows[:, 2 * model_width :]
     all_keys, all_values = (
         lax.all_gather(local_keys, ("gx", "gy"), axis=0, tiled=True),
-        lax.all_gather(local_values, ("gx", "gy"), axis=0, tiled=True),
+        jnp.concatenate(
+            lax.all_to_all(
+                jnp.stack([local_values] * lax.axis_size(("gx", "gy"))), ("gx", "gy"), 0, 0
+            ),
+            axis=0,
+        ),
     )
     queries_h = queries.reshape(tok_count, H, HD)
     keys_h = all_keys.reshape(-1, H, HD)

time: 593 us -> 556 us (0.938)
  waiting for transfers between devices: 341 us -> 297 us
    all_gather x1 -> x0, waiting for transfers between devices: 39.5 us -> none  [local(): lax.all_gather(local_values, ('gx', 'gy'), axis=0, tiled=True)]
    all_gather x1, waiting for transfers between devices: 49 us -> 16.3 us  [local(): lax.all_gather(local_keys, ('gx', 'gy'), axis=0, tiled=True)]
    all_to_all x0 -> x1, waiting for transfers between devices: none -> 28.7 us  [local(): lax.all_to_all(jnp.stack([local_values] * lax.axis_size(('gx', 'gy'))), (...]
    all_to_all x0 -> x1, starting transfers between devices: none -> 6.12 us  [local(): lax.all_to_all(jnp.stack([local_values] * lax.axis_size(('gx', 'gy'))), (...]
    another operation x0 -> x2, local copies, waits for them, and re-layouts: none -> 6.05 us  [the longest x1 4.31 us: local(): values_h = all_values.reshape(-1, H, HD)]
    unnamed x74 -> x72, local copies, waits for them, and re-layouts: 38.3 us -> 36 us
    unnamed x8 -> x7, waiting for transfers between devices: 57.5 us -> 58.4 us
  transfers between devices with their start and end apart: 15 -> 15, of which waited for: 10 -> 10; matrix products, arithmetic and copies ran while one was open for 14% -> 16% of each run, Pallas kernels for 0% -> 0%
where the time goes in v1:
time: 556 us; the launch traced here: 548 us
  waiting for transfers between devices  297 us (53%)
  local copies, waits for them, and re-layouts  94.4 us (17%)
  matrix products  72.6 us (13%)
  blocking collectives  30.3 us (5%)
  starting transfers between devices  19.7 us (4%)
  other arithmetic  17.8 us (3%)
  between operations  15.9 us (3%)
    reduce_scatter x1, waiting for transfers between devices, local(): lax.psum_scatter(conv_part.astype(jnp.bfloat16), ('gx', 'gy'), scatter_di...  74.3 us
    reduce_scatter x1, waiting for transfers between devices, local(): lax.psum_scatter(down_part.astype(jnp.bfloat16), ('gx', 'gy'), scatter_di...  69.4 us
    unnamed x7, waiting for transfers between devices  58.4 us
    reduce_scatter x1, waiting for transfers between devices, local(): lax.psum_scatter(qkv_part.astype(jnp.bfloat16), ('gx', 'gy'), scatter_dim...  42.7 us
    unnamed x72, local copies, waits for them, and re-layouts  36 us
    unnamed x1, blocking collectives  30.3 us
    all_to_all x1, waiting for transfers between devices, local(): lax.all_to_all(jnp.stack([local_values] * lax.axis_size(('gx', 'gy'))), (...  28.7 us
    reshape x1, local copies, waits for them, and re-layouts, gather_patches(): return joined.reshape(extent_x * extent_y * extent_z, 27 * channels)  22.7 us
  transfers between devices with their start and end apart: 15, of which 10 were waited for; matrix products, arithmetic and copies ran while one was open for 16% of the time, Pallas kernels for 0%

profile of v1, /device:TPU:16, one launch (start us, length us, event | category | flops | bytes accessed | tf_op | source)
XLA Modules:
  0.0 548.1 jit_solution(16050231064842160327)
XLA Ops:
  8.2 1.7 collective-permute-start
  9.9 1.3 collective-permute-start.1
  11.3 1.4 constant_dynamic-update-slice_fusion.1
  12.6 1.5 collective-permute-done.1
  14.1 3.4 collective-permute-start.2
  17.6 1.3 collective-permute-start.3
  19.2 4.2 collective-permute-done.3
  25.1 1.2 fusion.45
  26.3 1.2 slice_dynamic-update-slice_fusion.34
  28.6 2.2 fusion.61
  30.8 1.1 slice_dynamic-update-slice_fusion.32
  31.9 1.2 slice_dynamic-update-slice_fusion.31
  33.1 1.2 fusion.41
  34.3 1.1 slice_dynamic-update-slice_fusion.30
  35.4 1.2 slice_dynamic-update-slice_fusion.29
  41.0 1.2 slice_dynamic-update-slice_fusion.26
  43.3 1.2 fusion.39
  44.4 1.2 slice_dynamic-update-slice_fusion.24
  46.7 1.2 fusion.60
  50.1 1.2 fusion.59
  53.5 1.2 fusion.58
  54.7 1.1 slice_dynamic-update-slice_fusion.18
  55.9 22.7 %reshape.88 = bf16[1024,6912]{1,0:T(8,128)(2,1)} reshape(bf16[16,16,4,6912]{3,2,1,0:T(4,128)(2,1)} %slice_dynamic-update-slice_fusion.18) | data formatting | bytes 28311552 | tf_op jit(solution)/shard_map/reshape | solution.py:55
  78.6 10.9 %multiply_convert_fusion.2 = (bf16[1024,256]{1,0:T(8,128)(2,1)S(1)}, f32[1024,256]{1,0:T(8,128)}) fusion(bf16[1024,6912]{1,0:T(8,128)(2,1)} %reshape.88, bf16[6912,256]{1,0:T(8,128)(2,1)} %param.8), kind=kOutput, calls=%fused_computation.54 | convolution fusion | flops 3625189376 | bytes 19267584 | tf_op jit(solution)/shard_map/dot_general | solution.py:66
  91.2 1.8 convolution_convert_fusion.6
  93.9 1.7 stack.2
  95.6 6.1 %all-to-all-start = ((bf16[16,128,512]{1,2,0:T(8,128)(2,1)}), bf16[16,128,512]{1,2,0:T(8,128)(2,1)}, u32[]{:S(2)}, u32[]{:S(2)}) async-start(bf16[16,128,512]{1,2,0:T(8,128)(2,1)} %stack.2), calls=%async_computation | async-start | bytes 4194304 | tf_op jit(solution)/shard_map/all_to_all | solution.py:86
  102.8 1.3 convolution_convert_fusion.9
  104.4 28.7 %all-to-all-done = bf16[16,128,512]{1,2,0:T(8,128)(2,1)} async-done(((bf16[16,128,512]{1,2,0:T(8,128)(2,1)}), bf16[16,128,512]{1,2,0:T(8,128)(2,1)}, u32[]{:S(2)}, u32[]{:S(2)}) %all-to-all-start) | async-done | bytes 2097184 | tf_op jit(solution)/shard_map/all_to_all | solution.py:86
  133.1 4.3 copy.48
  137.4 4.3 reshape_reshape.8
  141.7 16.3 %all-gather.2.cloned.1.call-done = bf16[2048,512]{1,0:T(8,128)(2,1)} async-done(((bf16[128,512]{1,0:T(8,128)(2,1)}), bf16[2048,512]{1,0:T(8,128)(2,1)}) %all-gather.2.cloned.1.call-update) | async-done | bytes 2097168 | tf_op jit(solution)/shard_map/all_gather | solution.py:84
  158.0 3.9 copy.44
  162.0 3.1 fusion.3
  165.1 2.0 convolution_convert_fusion.4
  168.2 2.7 fusion
  171.0 5.9 %multiply_convert_fusion = bf16[8,64,2048]{2,1,0:T(8,128)(2,1)S(1)} fusion(bf16[128,8,64]{0,2,1:T(8,128)(2,1)S(1)} %bitcast.66, bf16[8,128,2048]{2,1,0:T(8,128)(2,1)S(1)} %get-tuple-element.47, f32[8,128]{1,0:T(8,128)S(1)} %get-tuple-element.46, f32[8,128,2048]{2,1,0:T(8,128)S(1)} %get-tuple-element.45, f32[8,128]{1,0:T(8,128)S(1)} %get-tuple-element.44), kind=kOutput, calls=%fused_computation.11 | convolution fusion | flops 1623195648 | bytes 14819328 | tf_op jit(solution)/shard_map/hij,ihe->jhe/dot_general | solution.py:123
  176.8 2.5 pad_maximum_fusion
  179.4 6.4 %copy.59 = bf16[2048,1024]{1,0:T(8,128)(2,1)} copy(bf16[2048,1024]{0,1:T(8,128)(2,1)} %pad_maximum_fusion) | data formatting | bytes 8388608
  185.8 5.7 %fusion.31 = bf16[8,64,128]{2,1,0:T(8,128)(2,1)S(1)} fusion(bf16[2048,8,64]{0,2,1:T(8,128)(2,1)} %reshape_reshape.8, f32[8,128,2048]{2,1,0:T(8,128)} %copy-done.2, f32[8,128]{1,0:T(8,128)S(1)} %get-tuple-element.44), kind=kOutput, calls=%fused_computation.47 | convolution fusion | flops 274792448 | bytes 10620928 | tf_op jit(solution)/shard_map/hij,jhe->ihe/dot_general | solution.py:103
  193.0 11.9 %fusion.34 = bf16[8,64,128]{2,1,0:T(8,128)(2,1)S(1)} fusion(bf16[2048,8,64]{0,2,1:T(8,128)(2,1)} %bitcast.58, bf16[8,128,2048]{2,1,0:T(8,128)(2,1)} %copy-done.13, f32[8,128]{1,0:T(8,128)S(1)} %get-tuple-element.46, f32[8,128,2048]{2,1,0:T(8,128)} %copy-done.2, f32[8,128]{1,0:T(8,128)S(1)} %get-tuple-element.44), kind=kOutput, calls=%fused_computation.49 | convolution fusion | flops 1621229568 | bytes 14819328 | tf_op jit(solution)/shard_map/hij,jhe->ihe/dot_general | solution.py:117
  204.9 58.3 %reduce-scatter.16.cloned.1.call-done = bf16[128,1024]{1,0:T(8,128)(2,1)} async-done(((bf16[2048,1024]{1,0:T(8,128)(2,1)}), bf16[128,1024]{1,0:T(8,128)(2,1)}) %reduce-scatter.16.cloned.1.call-update) | async-done | bytes 262160
  264.3 1.8 convolution_convert_fusion.3
  266.2 2.8 multiply_reduce_fusion
  269.0 3.3 convolution_convert_fusion.2
  272.7 3.1 fusion.14
  275.8 1.9 reshape.99
  277.7 2.7 copy.66
  280.4 1.9 reshape.98
  282.3 1.6 multiply_convert_fusion.1
  284.8 1.3 collective-permute-start.4
  286.1 5.7 %copy.56 = bf16[27,256,256]{2,1,0:T(8,128)(2,1)} copy(bf16[27,256,256]{1,2,0:T(8,128)(2,1)} %bitcast.60) | data formatting | bytes 7077888 | tf_op jit(solution)/shard_map/transpose | solution.py:184
  293.0 2.0 reshape.95
  295.1 1.3 collective-permute-start.5
  296.4 1.2 fusion.70
  297.6 1.6 collective-permute-done.5
  299.9 1.3 collective-permute-start.6
  301.2 1.3 collective-permute-start.7
  302.5 10.8 %convolution_convert_fusion = bf16[6912,256]{1,0:T(8,128)(2,1)} fusion(bf16[1024,6912]{1,0:T(8,128)(2,1)} %reshape.88, bf16[1024,256]{1,0:T(8,128)(2,1)} %copy-done.5), kind=kOutput, calls=%fused_computation.2 | convolution fusion | flops 3625648128 | bytes 18219008 | tf_op jit(solution)/shard_map/vr,vc->rc/dot_general | solution.py:176
  313.3 30.3 %all-reduce.2 = f32[512]{0:T(512)S(1)} all-reduce(f32[512]{0:T(512)S(1)} %copy-done.11), channel_id=5, replica_groups=mesh['batch'=16,'gx'=4,'gy'=4] {'gx','gy'}, use_global_device_ids=true, to_apply=%region_10.11.clone | all-reduce | flops 512 | bytes 4096
  349.5 3.8 convolution_convert_fusion.7
  354.4 42.7 %reduce-scatter.12.cloned.1.call-done = bf16[32,1536]{1,0:T(8,128)(2,1)} async-done(((bf16[512,1536]{1,0:T(8,128)(2,1)}), bf16[32,1536]{1,0:T(8,128)(2,1)}) %reduce-scatter.12.cloned.1.call-update) | async-done | bytes 98320 | tf_op jit(solution)/shard_map/reduce_scatter | solution.py:198
  397.1 69.4 %reduce-scatter.10.cloned.1.call-done = bf16[128,512]{1,0:T(8,128)(2,1)} async-done(((bf16[2048,512]{1,0:T(8,128)(2,1)}), bf16[128,512]{1,0:T(8,128)(2,1)}) %reduce-scatter.10.cloned.1.call-update) | async-done | bytes 131088 | tf_op jit(solution)/shard_map/reduce_scatter | solution.py:195
  466.5 74.3 %reduce-scatter.8.cloned.1.call-done = bf16[432,256]{1,0:T(8,128)(2,1)} async-done(((bf16[6912,256]{1,0:T(8,128)(2,1)}), bf16[432,256]{1,0:T(8,128)(2,1)}) %reduce-scatter.8.cloned.1.call-update) | async-done | bytes 221200 | tf_op jit(solution)/shard_map/reduce_scatter | solution.py:192
  (117 shorter events, 32.1 us)
Async XLA Ops:
  7.2 83.3 %copy-start = (bf16[2048,512]{1,0:T(8,128)(2,1)S(1)}, bf16[2048,512]{1,0:T(8,128)(2,1)}, u32[]{:S(2)}) copy-start(bf16[2048,512]{1,0:T(8,128)(2,1)} %param.9) | copy-start | bytes 6291460
  7.2 150.8 %all-gather.2.cloned.1.call-start = ((), (), s32[]{:S(2)}) async-start(), calls=%async_computation.6 | async-start | bytes 2228224 | tf_op jit(solution)/shard_map/all_gather | solution.py:84
  8.2 3.1 collective-permute-start
  9.9 4.2 collective-permute-start.1
  11.2 28.7 %copy-start.1 = (bf16[16,16,4,256]{3,2,1,0:T(4,128)(2,1)S(1)}, bf16[16,16,4,256]{3,2,1,0:T(4,128)(2,1)}, u32[]{:S(2)}) copy-start(bf16[16,16,4,256]{3,2,1,0:T(4,128)(2,1)} %param.7) | copy-start | bytes 1572868
  14.1 5.0 collective-permute-start.2
  17.6 5.9 %collective-permute-start.3 = (bf16[18,1,4,256]{3,2,1,0:T(4,128)(2,1)S(1)}, bf16[18,1,4,256]{3,2,1,0:T(4,128)(2,1)S(1)}, u32[]{:S(2)}, u32[]{:S(2)}) collective-permute-start(bf16[18,1,4,256]{3,2,1,0:T(4,128)(2,1)S(1)} %get-tuple-element.30), channel_id=1, source_target_pairs={{1,0},{2,1},{3,2},{5,4},{6,5},{7,6},{9,8},{10,9},{11,10},{13,12},{... | collective-permute-start | bytes 110600 | tf_op jit(solution)/shard_map/ppermute | solution.py:19
  78.6 12.6 %copy-start.9 = (f32[512]{0:T(512)S(1)}, f32[512]{0:T(512)}, u32[]{:S(2)}) copy-start(f32[512]{0:T(512)} %param.10) | copy-start | bytes 6148
  95.6 37.5 %all-to-all-start = ((bf16[16,128,512]{1,2,0:T(8,128)(2,1)}), bf16[16,128,512]{1,2,0:T(8,128)(2,1)}, u32[]{:S(2)}, u32[]{:S(2)}) async-start(bf16[16,128,512]{1,2,0:T(8,128)(2,1)} %stack.2), calls=%async_computation | async-start | bytes 4194304 | tf_op jit(solution)/shard_map/all_to_all | solution.py:86
  101.7 161.4 %reduce-scatter.16.cloned.1.call-start = ((), (), s32[]{:S(2)}) async-start(), calls=%async_computation.11 | async-start | bytes 4456448
  165.1 5.9 %copy-start.2 = (f32[8,128,2048]{2,1,0:T(8,128)}, f32[8,128,2048]{2,1,0:T(8,128)S(1)}, u32[]{:S(2)}) copy-start(f32[8,128,2048]{2,1,0:T(8,128)S(1)} %get-tuple-element.45) | copy-start | bytes 25165828
  165.1 3.1 copy-start.6
  170.9 5.9 %copy-start.13 = (bf16[8,128,2048]{2,1,0:T(8,128)(2,1)}, bf16[8,128,2048]{2,1,0:T(8,128)(2,1)S(1)}, u32[]{:S(2)}) copy-start(bf16[8,128,2048]{2,1,0:T(8,128)(2,1)S(1)} %get-tuple-element.47) | copy-start | bytes 12582916
  185.8 168.6 %reduce-scatter.14.cloned.1.call-start = ((), (), s32[]{:S(2)}) async-start(), calls=%async_computation.10 | async-start | bytes 557056 | tf_op jit(solution)/shard_map/reduce_scatter | solution.py:201
  192.7 204.4 %reduce-scatter.12.cloned.1.call-start = ((), (), s32[]{:S(2)}) async-start(), calls=%async_computation.9 | async-start | bytes 1671168 | tf_op jit(solution)/shard_map/reduce_scatter | solution.py:198
  204.8 61.3 %copy-start.8 = (bf16[8,64,128]{2,1,0:T(8,128)(2,1)}, bf16[8,64,128]{2,1,0:T(8,128)(2,1)S(1)}, u32[]{:S(2)}) copy-start(bf16[8,64,128]{2,1,0:T(8,128)(2,1)S(1)} %fusion.34) | copy-start | bytes 393220
  266.1 200.4 %reduce-scatter.10.cloned.1.call-start = ((), (), s32[]{:S(2)}) async-start(), calls=%async_computation.8 | async-start | bytes 2228224 | tf_op jit(solution)/shard_map/reduce_scatter | solution.py:195
  269.0 3.4 copy-start.7
  269.0 3.4 copy-start.10
  272.4 268.4 %reduce-scatter.8.cloned.1.call-start = ((), (), s32[]{:S(2)}) async-start(), calls=%async_computation.7 | async-start | bytes 3760128 | tf_op jit(solution)/shard_map/reduce_scatter | solution.py:192
  275.8 16.0 %copy-start.12 = (u32[256]{0:T(256)S(1)}, u32[256]{0:T(256)}, u32[]{:S(2)}) copy-start(u32[256]{0:T(256)} %constant.27) | copy-start | bytes 3076
  283.9 0.8 copy-start.5
  284.8 11.6 %collective-permute-start.4 = (bf16[1,16,4,256]{3,1,2,0:T(8,128)(2,1)S(1)}, bf16[1,16,4,256]{3,1,2,0:T(8,128)(2,1)S(1)}, u32[]{:S(2)}, u32[]{:S(2)}) collective-permute-start(bf16[1,16,4,256]{3,1,2,0:T(8,128)(2,1)S(1)} %copy.50), channel_id=1, source_target_pairs={{0,4},{4,8},{8,12},{1,5},{5,9},{9,13},{2,6},{6,10},{10,14},{3,7},{... | collective-permute-start | bytes 98312 | tf_op jit(solution)/shard_map/ppermute | solution.py:16
  295.1 4.1 collective-permute-start.5
  299.9 44.2 %collective-permute-start.6 = (bf16[18,1,4,256]{3,1,2,0:T(2,128)(2,1)}, bf16[18,1,4,256]{3,1,2,0:T(2,128)(2,1)S(1)}, u32[]{:S(2)}, u32[]{:S(2)}) collective-permute-start(bf16[18,1,4,256]{3,1,2,0:T(2,128)(2,1)} %get-tuple-element.27), channel_id=1, source_target_pairs={{0,1},{1,2},{2,3},{4,5},{5,6},{6,7},{8,9},{9,10},{10,11},{12,13},{... | collective-permute-start | bytes 110600 | tf_op jit(solution)/shard_map/ppermute | solution.py:16
  301.2 12.1 %copy-start.11 = (f32[512]{0:T(512)S(1)}, f32[512]{0:T(512)}, u32[]{:S(2)}) copy-start(f32[512]{0:T(512)} %get-tuple-element.24) | copy-start | bytes 6148
  301.2 42.9 %collective-permute-start.7 = (bf16[18,1,4,256]{3,1,2,0:T(2,128)(2,1)S(1)}, bf16[18,1,4,256]{3,1,2,0:T(2,128)(2,1)S(1)}, u32[]{:S(2)}, u32[]{:S(2)}) collective-permute-start(bf16[18,1,4,256]{3,1,2,0:T(2,128)(2,1)S(1)} %get-tuple-element.28), channel_id=1, source_target_pairs={{1,0},{2,1},{3,2},{5,4},{6,5},{7,6},{9,8},{10,9},{11,10},{13,12},{... | collective-permute-start | bytes 110600 | tf_op jit(solution)/shard_map/ppermute | solution.py:19
  343.6 3.7 copy-start.3
  346.9 2.6 copy-start.4
Sparse Core Ops, SparseCore 0:
  93.9 64.0 all-gather.1
  185.9 77.1 reduce-scatter.15
  266.2 62.6 reduce-scatter.13
  331.8 65.2 reduce-scatter.11
  400.0 66.4 reduce-scatter.9
  469.5 71.2 reduce-scatter.7
